TPU v7x, 128 devices: a whole 4x4x4 slice. The times are simulated.
128 devices in a mesh: seq: 16 (over z, y), tp: 8 (over x, core).
Axes of the slice: x: 4, y: 4, z: 4, core: 2. Of those that a mesh axis runs over, the one named last changes fastest.
Arguments:
- tokens: bfloat16 [8192, 4096], P(('seq', 'tp')), may hold values from -24 to 24
- w_query: bfloat16 [4096, 4096], P(None, 'tp'), may hold values from -0.09375 to 0.09375
- w_key: bfloat16 [4096, 4096], P(None, 'tp'), may hold values from -0.09375 to 0.09375
- w_value: bfloat16 [4096, 4096], P(None, 'tp'), may hold values from -0.09375 to 0.09375
- w_out: bfloat16 [4096, 4096], P('tp'), may hold values from -0.09375 to 0.09375
- state_in: float32 [32, 128, 128], P('tp'), may hold values from -400 to 400
- grad_out: bfloat16 [8192, 4096], P(('seq', 'tp')), may hold values from -6 to 6
Outputs:
- mixed_out: bfloat16 [8192, 4096], P(('seq', 'tp'))
- input_grad: bfloat16 [8192, 4096], P(('seq', 'tp'))
- query_wgrad: float32 [4096, 4096], P('seq', 'tp')
- key_wgrad: float32 [4096, 4096], P('seq', 'tp')
- value_wgrad: float32 [4096, 4096], P('seq', 'tp')
- out_wgrad: float32 [4096, 4096], P('tp', 'seq')
- state_grad: float32 [32, 128, 128], P('tp', 'seq')
All inputs are finite; a program needn't handle non-finite values.
Results may differ from a plain program's by a relative error of at most 0.02.
Values may be sent and summed in bfloat16 or wider, within the bound.
No kernel may reach another device: no remote copies, remote signals or barrier semaphores. Data moves between devices by JAX's collectives and lax.ppermute only.
A program may use at most 128 MiB of HBM per device.

v0:
```python
import jax
import jax.numpy as jnp
from jax import lax
from jax.sharding import PartitionSpec as P

HIGH = lax.Precision.HIGHEST
ROWS_CONTRACT = (((0,), (0,)), ((), ()))
COLS_CONTRACT = (((1,), (1,)), ((), ()))


def carried_in(array, axis, join, neutral, backward):
    count = lax.axis_size(axis)
    place = lax.axis_index(axis)
    ahead = count - 1 - place if backward else place
    gathered = lax.all_gather(array.astype(jnp.bfloat16), axis)
    state = jnp.zeros_like(array) + jnp.asarray(neutral, array.dtype)

    def one(hop, state):
        source = count - 1 - hop if backward else hop
        return join(state, lax.dynamic_index_in_dim(gathered, source, 0, False).astype(array.dtype))

    return lax.fori_loop(0, ahead, one, state)


def add_states(earlier, later):
    return earlier + later


def body(tokens, w_query, w_key, w_value, w_out, state_in, grad_out):
    head_count = state_in.shape[0]
    head_width = state_in.shape[1]
    rows_all = lax.all_gather(tokens, "tp", axis=0, tiled=True)
    shard_len = rows_all.shape[0]

    def head_split(matrix):
        return matrix.reshape(shard_len, head_count, head_width)

    query = jnp.dot(rows_all, w_query, preferred_element_type=jnp.float32).astype(jnp.bfloat16)
    key_all = jnp.dot(rows_all, w_key, preferred_element_type=jnp.float32).astype(jnp.bfloat16)
    value_all = jnp.dot(rows_all, w_value, preferred_element_type=jnp.float32).astype(jnp.bfloat16)
    query_heads = head_split(query)
    key_heads = head_split(key_all)
    value_heads = head_split(value_all)
    query_full = query_heads.astype(jnp.float32)
    key_full = key_heads.astype(jnp.float32)
    value_full = value_heads.astype(jnp.float32)
    local_kv = jnp.einsum(
        "thd,the->hde", key_heads, value_heads, preferred_element_type=jnp.float32
    )
    empty_state = jnp.zeros_like(local_kv)
    earlier = carried_in(local_kv, "seq", add_states, empty_state, False)
    state_before = state_in + earlier
    row_ids = lax.broadcasted_iota(jnp.int32, (shard_len, shard_len), 0)
    col_ids = lax.broadcasted_iota(jnp.int32, (shard_len, shard_len), 1)
    mask = (row_ids >= col_ids)[None]
    scores = jnp.einsum("thd,shd->hts", query_heads, key_heads, preferred_element_type=jnp.float32)
    masked = jnp.where(mask, scores, 0.0)
    attn = jnp.einsum("hts,shd->thd", masked, value_full, precision=HIGH) + jnp.einsum(
        "thd,hde->the", query_full, state_before, precision=HIGH
    )
    inverse = lax.rsqrt(jnp.mean(attn * attn, axis=-1, keepdims=True) + 1e-05)
    normed = attn * inverse
    heads_out = normed.reshape(shard_len, head_count * head_width).astype(jnp.bfloat16)
    mixed_out = lax.psum_scatter(
        jnp.dot(heads_out, w_out, preferred_element_type=jnp.float32).astype(jnp.bfloat16),
        "tp",
        scatter_dimension=0,
        tiled=True,
    )
    grad_all = lax.all_gather(grad_out, "tp", axis=0, tiled=True)
    out_part = lax.dot_general(
        heads_out, grad_all, ROWS_CONTRACT, preferred_element_type=jnp.float32
    )
    d_normed = lax.dot_general(grad_all, w_out, COLS_CONTRACT, preferred_element_type=jnp.float32)
    d_normed = d_normed.reshape(shard_len, head_count, head_width)
    d_attn = inverse * (d_normed - normed * jnp.mean(d_normed * normed, axis=-1, keepdims=True))
    local_adj = jnp.einsum("thd,the->hde", query_full, d_attn, precision=HIGH)
    later = carried_in(local_adj, "seq", add_states, empty_state, True)
    state_grad = lax.psum_scatter(
        local_adj.astype(jnp.bfloat16), "seq", scatter_dimension=1, tiled=True
    ).astype(jnp.float32)
    mixed_s = jnp.where(mask, jnp.einsum("the,she->hts", d_attn, value_full, precision=HIGH), 0.0)
    grad_q = jnp.einsum("the,hde->thd", d_attn, state_before, precision=HIGH) + jnp.einsum(
        "hts,shd->thd", mixed_s, key_full, precision=HIGH
    )
    grad_k = jnp.einsum("hts,thd->shd", mixed_s, query_full, precision=HIGH) + jnp.einsum(
        "hde,she->shd", later, value_full, precision=HIGH
    )
    grad_v = jnp.einsum("hts,the->she", masked, d_attn, precision=HIGH) + jnp.einsum(
        "hde,shd->she", later, key_full, precision=HIGH
    )
    query_grad = grad_q.reshape(shard_len, head_count * head_width).astype(jnp.bfloat16)
    key_grad = grad_k.reshape(shard_len, head_count * head_width).astype(jnp.bfloat16)
    value_grad = grad_v.reshape(shard_len, head_count * head_width).astype(jnp.bfloat16)
    term = lax.dot_general(query_grad, w_query, COLS_CONTRACT, preferred_element_type=jnp.float32)
    term = term + lax.dot_general(
        key_grad, w_key, COLS_CONTRACT, preferred_element_type=jnp.float32
    )
    input_grad = lax.psum_scatter(
        (
            term
            + lax.dot_general(
                value_grad, w_value, COLS_CONTRACT, preferred_element_type=jnp.float32
            )
        ).astype(jnp.bfloat16),
        "tp",
        scatter_dimension=0,
        tiled=True,
    )
    query_part = lax.dot_general(
        rows_all, query_grad, ROWS_CONTRACT, preferred_element_type=jnp.float32
    )
    key_part = lax.dot_general(
        rows_all, key_grad, ROWS_CONTRACT, preferred_element_type=jnp.float32
    )
    value_part = lax.dot_general(
        rows_all, value_grad, ROWS_CONTRACT, preferred_element_type=jnp.float32
    )
    query_sum, key_sum, value_sum, out_summed = (
        lax.psum_scatter(
            query_part.astype(jnp.bfloat16), "seq", scatter_dimension=0, tiled=True
        ).astype(jnp.float32),
        lax.psum_scatter(
            key_part.astype(jnp.bfloat16), "seq", scatter_dimension=0, tiled=True
        ).astype(jnp.float32),
        lax.psum_scatter(
            value_part.astype(jnp.bfloat16), "seq", scatter_dimension=0, tiled=True
        ).astype(jnp.float32),
        lax.psum_scatter(
            out_part.astype(jnp.bfloat16), "seq", scatter_dimension=1, tiled=True
        ).astype(jnp.float32),
    )
    grad_scale = lax.rsqrt(jnp.float32(shard_len * lax.axis_size("seq")))
    return (
        mixed_out,
        input_grad,
        query_sum * grad_scale,
        key_sum * grad_scale,
        value_sum * grad_scale,
        out_summed * grad_scale,
        state_grad,
    )


def solution(mesh):
    return jax.shard_map(
        body,
        mesh=mesh,
        in_specs=(
            P(("seq", "tp"), None),
            P(None, "tp"),
            P(None, "tp"),
            P(None, "tp"),
            P("tp", None),
            P("tp", None, None),
            P(("seq", "tp"), None),
        ),
        out_specs=(
            P(("seq", "tp"), None),
            P(("seq", "tp"), None),
            P("seq", "tp"),
            P("seq", "tp"),
            P("seq", "tp"),
            P("tp", "seq"),
            P("tp", "seq", None),
        ),
        check_vma=False,
    )
```

profile of v0, /device:TPU:0, one launch (start us, length us, event | category | flops | bytes accessed | tf_op | source)
XLA Modules:
  0.0 680.8 jit_solution(14253382885629897985)
XLA Ops:
  7.9 36.3 %all-gather.7.cloned.1.call-done = bf16[512,4096]{1,0:T(8,128)(2,1)} async-done(((bf16[64,4096]{1,0:T(8,128)(2,1)}), bf16[512,4096]{1,0:T(8,128)(2,1)}) %all-gather.7.cloned.1.call-update) | async-done | bytes 4194320 | tf_op jit(solution)/shard_map/all_gather | solution.py:32
  44.3 6.0 convolution_convert_fusion.5
  54.5 5.8 convolution_convert_fusion.6
  63.2 35.9 %all-gather.11.cloned.1.call-done = bf16[64,128,128]{2,1,0:T(8,128)(2,1)} async-done(((bf16[4,128,128]{2,1,0:T(8,128)(2,1)}), bf16[64,128,128]{2,1,0:T(8,128)(2,1)}) %all-gather.11.cloned.1.call-update) | async-done | bytes 2097168 | tf_op jit(solution)/shard_map/all_gather | solution.py:15
  100.3 5.0 multiply_reduce_fusion.1
  105.3 26.9 %all-gather.9.cloned.1.call-done = bf16[512,4096]{1,0:T(8,128)(2,1)} async-done(((bf16[64,4096]{1,0:T(8,128)(2,1)}), bf16[512,4096]{1,0:T(8,128)(2,1)}) %all-gather.9.cloned.1.call-update) | async-done | bytes 4194320 | tf_op jit(solution)/shard_map/all_gather | solution.py:70
  132.2 5.8 multiply_reduce_fusion
  150.2 35.7 %all-gather.13.cloned.1.call-done = bf16[64,128,128]{2,1,0:T(8,128)(2,1)} async-done(((bf16[4,128,128]{2,1,0:T(8,128)(2,1)}), bf16[64,128,128]{2,1,0:T(8,128)(2,1)}) %all-gather.13.cloned.1.call-update) | async-done | bytes 2097168 | tf_op jit(solution)/shard_map/all_gather | solution.py:15
  186.7 6.5 fusion
  194.2 6.5 convolution_convert_fusion
  200.8 14.8 %while.23 = (s32[]{:T(128)}, f32[4,128,128]{2,1,0:T(8,128)S(1)}, s32[]{:T(128)}, bf16[16,4,128,128]{3,2,1,0:T(8,128)(2,1)}, s32[]{:T(128)}, /*index=5*/s32[]{:T(128)}, s32[]{:T(128)}, s32[]{:T(128)}) while((s32[]{:T(128)}, f32[4,128,128]{2,1,0:T(8,128)S(1)}, s32[]{:T(128)}, bf16[16,4,128,128]{3,2,1,0:T(8,128)(2,1)}, s32[]{:T(128)}, ...), condition=%wide.region_6.7_spmd, body=%wide.region_5.6_spmd.sunk | while | flops 131078 | bytes 655503 | solution.py:22
  216.3 4.4 fusion.39
  225.4 5.1 fusion.35
  237.3 6.6 convolution_convert_fusion.4
  244.9 4.7 fusion.53
  249.7 5.7 fusion.54
  255.4 7.8 %add_convert_fusion = bf16[512,4096]{1,0:T(8,128)(2,1)} fusion(f32[512,4096]{1,0:T(8,128)S(1)} %fusion.53, f32[512,4096]{1,0:T(8,128)} %fusion.54, bf16[512,512]{0,1:T(8,128)(2,1)S(1)} %bitcast.114, bf16[4096,512]{1,0:T(8,128)(2,1)S(1)} %copy-done.5), kind=kOutput, calls=%fused_computation.2 | convolution fusion | flops 2153775104 | bytes 25690112 | tf_op jit(solution)/shard_map/dot_general | solution.py:102
  265.1 6.7 all-reduce.3.cloned.1.call-done
  273.1 79.3 %reduce-scatter.12.cloned.1.call-done = bf16[256,512]{0,1:T(8,128)(2,1)} async-done(((bf16[4096,512]{0,1:T(8,128)(2,1)}), bf16[256,512]{0,1:T(8,128)(2,1)}) %reduce-scatter.12.cloned.1.call-update) | async-done | bytes 262160 | tf_op jit(solution)/shard_map/reduce_scatter | solution.py:120
  354.4 78.4 %reduce-scatter.18.cloned.1.call-done = bf16[512,256]{1,0:T(8,128)(2,1)} async-done(((bf16[512,4096]{1,0:T(8,128)(2,1)}), bf16[512,256]{1,0:T(8,128)(2,1)}) %reduce-scatter.18.cloned.1.call-update) | async-done | bytes 262160 | tf_op jit(solution)/shard_map/reduce_scatter | solution.py:129
  434.6 78.9 %reduce-scatter.14.cloned.1.call-done = bf16[256,512]{0,1:T(8,128)(2,1)} async-done(((bf16[4096,512]{0,1:T(8,128)(2,1)}), bf16[256,512]{0,1:T(8,128)(2,1)}) %reduce-scatter.14.cloned.1.call-update) | async-done | bytes 262160 | tf_op jit(solution)/shard_map/reduce_scatter | solution.py:123
  515.5 78.4 %reduce-scatter.16.cloned.1.call-done = bf16[256,512]{0,1:T(8,128)(2,1)} async-done(((bf16[4096,512]{0,1:T(8,128)(2,1)}), bf16[256,512]{0,1:T(8,128)(2,1)}) %reduce-scatter.16.cloned.1.call-update) | async-done | bytes 262160 | tf_op jit(solution)/shard_map/reduce_scatter | solution.py:126
  595.9 38.0 %reduce-scatter.8.cloned.1.call-done = bf16[64,4096]{1,0:T(8,128)(2,1)} async-done(((bf16[512,4096]{1,0:T(8,128)(2,1)}), bf16[64,4096]{1,0:T(8,128)(2,1)}) %reduce-scatter.8.cloned.1.call-update) | async-done | bytes 524304 | tf_op jit(solution)/shard_map/reduce_scatter | solution.py:64
  633.9 40.1 %reduce-scatter.10.cloned.1.call-done = bf16[64,4096]{1,0:T(8,128)(2,1)} async-done(((bf16[512,4096]{1,0:T(8,128)(2,1)}), bf16[64,4096]{1,0:T(8,128)(2,1)}) %reduce-scatter.10.cloned.1.call-update) | async-done | bytes 524304 | tf_op jit(solution)/shard_map/reduce_scatter | solution.py:99
  (106 shorter events, 60.7 us)
Async XLA Ops:
  7.2 37.1 %all-gather.7.cloned.1.call-start = ((), (), s32[]{:S(2)}) async-start(), calls=%async_computation.6 | async-start | bytes 4718592 | tf_op jit(solution)/shard_map/all_gather | solution.py:32
  7.9 91.2 %all-gather.11.cloned.1.call-start = ((), (), s32[]{:S(2)}) async-start(), calls=%async_computation.14 | async-start | bytes 2228224 | tf_op jit(solution)/shard_map/all_gather | solution.py:15
  44.3 6.0 copy-start.4
  44.3 6.0 copy-start.16
  52.7 47.6 %copy-start.1 = (bf16[512,512]{0,1:T(8,128)(2,1)}, bf16[512,512]{0,1:T(8,128)(2,1)S(1)}, u32[]{:S(2)}) copy-start(bf16[512,512]{0,1:T(8,128)(2,1)S(1)} %convolution_convert_fusion.7) | copy-start | bytes 1572868
  53.7 78.5 %all-gather.9.cloned.1.call-start = ((), (), s32[]{:S(2)}) async-start(), calls=%async_computation.8 | async-start | bytes 4718592 | tf_op jit(solution)/shard_map/all_gather | solution.py:70
  54.4 131.5 %all-gather.13.cloned.1.call-start = ((), (), s32[]{:S(2)}) async-start(), calls=%async_computation.15 | async-start | bytes 2228224 | tf_op jit(solution)/shard_map/all_gather | solution.py:15
  60.4 39.2 %copy-start.15 = (f32[4,128,128]{2,1,0:T(8,128)S(1)}, f32[4,128,128]{2,1,0:T(8,128)}, u32[]{:S(2)}) copy-start(f32[4,128,128]{2,1,0:T(8,128)} %param.16) | copy-start | bytes 786436
  99.6 5.6 copy-start.6
  150.1 36.5 %copy-start.9 = (bf16[4,128,512]{2,1,0:T(8,128)(2,1)}, bf16[4,128,512]{2,1,0:T(8,128)(2,1)S(1)}, u32[]{:S(2)}) copy-start(bf16[4,128,512]{2,1,0:T(8,128)(2,1)S(1)} %fusion.42) | copy-start | bytes 1572868
  185.9 86.0 %all-reduce.3.cloned.1.call-start = ((), (), s32[]{:S(2)}) async-start(), calls=%async_computation.16 | async-start | bytes 262144
  186.4 166.0 %reduce-scatter.12.cloned.1.call-start = ((), (), s32[]{:S(2)}) async-start(), calls=%async_computation.10 | async-start | bytes 4456448 | tf_op jit(solution)/shard_map/reduce_scatter | solution.py:120
  193.2 239.6 %reduce-scatter.18.cloned.1.call-start = ((), (), s32[]{:S(2)}) async-start(), calls=%async_computation.13 | async-start | bytes 4456448 | tf_op jit(solution)/shard_map/reduce_scatter | solution.py:129
  200.7 15.0 %copy-start.2 = (bf16[512,512]{0,1:T(8,128)(2,1)S(1)}, bf16[512,512]{0,1:T(8,128)(2,1)}, u32[]{:S(2)}) copy-start(bf16[512,512]{0,1:T(8,128)(2,1)} %copy-done.1) | copy-start | bytes 1572868
  200.7 312.8 %reduce-scatter.14.cloned.1.call-start = ((), (), s32[]{:S(2)}) async-start(), calls=%async_computation.11 | async-start | bytes 4456448 | tf_op jit(solution)/shard_map/reduce_scatter | solution.py:123
  215.7 5.1 copy-start.17
  225.1 368.8 %reduce-scatter.16.cloned.1.call-start = ((), (), s32[]{:S(2)}) async-start(), calls=%async_computation.12 | async-start | bytes 4456448 | tf_op jit(solution)/shard_map/reduce_scatter | solution.py:126
  225.3 6.5 copy-start.18
  236.3 397.6 %reduce-scatter.8.cloned.1.call-start = ((), (), s32[]{:S(2)}) async-start(), calls=%async_computation.7 | async-start | bytes 4718592 | tf_op jit(solution)/shard_map/reduce_scatter | solution.py:64
  243.9 5.8 copy-start.12
  243.9 430.0 %reduce-scatter.10.cloned.1.call-start = ((), (), s32[]{:S(2)}) async-start(), calls=%async_computation.9 | async-start | bytes 4718592 | tf_op jit(solution)/shard_map/reduce_scatter | solution.py:99
  244.9 4.8 copy-start.3
  249.7 5.7 copy-start.5
  249.7 5.7 copy-start.14
  (7 other events, 10.9 us)
Sparse Core Ops, SparseCore 0:
  9.7 34.5 all-gather.6
  53.8 45.2 all-gather.10
  100.8 31.2 all-gather.8
  140.6 45.2 all-gather.12
  190.1 81.6 all-reduce.2
  275.4 77.0 reduce-scatter.11
  355.8 77.0 reduce-scatter.17
  436.5 76.9 reduce-scatter.13
  516.8 76.9 reduce-scatter.15
  596.8 36.9 reduce-scatter.7
  637.0 36.9 reduce-scatter.9
where the time goes:
time: 688 us; the launch traced here: 681 us
  waiting for transfers between devices  537 us (78%)
  matrix products  95.6 us (14%)
  other arithmetic  21.8 us (3%)
  between operations  15.1 us (2%)
  local copies, waits for them, and re-layouts  9.74 us (1%)
    reduce_scatter x1, waiting for transfers between devices, body(): lax.psum_scatter(query_part.astype(jnp.bfloat16), 'seq', scatter_dimensio...  79.3 us
    reduce_scatter x1, waiting for transfers between devices, body(): lax.psum_scatter(key_part.astype(jnp.bfloat16), 'seq', scatter_dimension=...  78.9 us
    reduce_scatter x1, waiting for transfers between devices, body(): lax.psum_scatter(value_part.astype(jnp.bfloat16), 'seq', scatter_dimensio...  78.4 us
    reduce_scatter x1, waiting for transfers between devices, body(): lax.psum_scatter(out_part.astype(jnp.bfloat16), 'seq', scatter_dimension=...  78.4 us
    all_gather x2, waiting for transfers between devices, carried_in(): gathered = lax.all_gather(array.astype(jnp.bfloat16), axis)  71.6 us
    reduce_scatter x1, waiting for transfers between devices, body(): lax.psum_scatter((term + lax.dot_general(value_grad, w_value, COLS_CONTRA...  40.1 us
    reduce_scatter x1, waiting for transfers between devices, body(): lax.psum_scatter(jnp.dot(heads_out, w_out, preferred_element_type=jnp.flo...  38 us
    all_gather x1, waiting for transfers between devices, body(): rows_all = lax.all_gather(tokens, 'tp', axis=0, tiled=True)  36.3 us
  transfers between devices with their start and end apart: 11, of which 11 were waited for; matrix products, arithmetic and copies ran while one was open for 15% of the time, Pallas kernels for 0%

commit v1 on v0

--- a/solution.py
+++ b/solution.py
@@ -8,22 +8,22 @@
 COLS_CONTRACT = (((1,), (1,)), ((), ()))
 
 
-def carried_in(array, axis, join, neutral, backward):
+def scanned(array, axis):
     count = lax.axis_size(axis)
     place = lax.axis_index(axis)
-    ahead = count - 1 - place if backward else place
-    gathered = lax.all_gather(array.astype(jnp.bfloat16), axis)
-    state = jnp.zeros_like(array) + jnp.asarray(neutral, array.dtype)
-
-    def one(hop, state):
-        source = count - 1 - hop if backward else hop
-        return join(state, lax.dynamic_index_in_dim(gathered, source, 0, False).astype(array.dtype))
-
-    return lax.fori_loop(0, ahead, one, state)
-
-
-def add_states(earlier, later):
-    return earlier + later
+    total = array
+    before = jnp.zeros_like(array)
+    after = jnp.zeros_like(array)
+    step = 1
+    while step < count:
+        pairs = [(i, i ^ step) for i in range(count)]
+        other = lax.ppermute(total, axis, pairs)
+        upper = (place & step) != 0
+        before = before + jnp.where(upper, other, 0.0)
+        after = after + jnp.where(upper, 0.0, other)
+        total = total + other
+        step *= 2
+    return before, after, total
 
 
 def body(tokens, w_query, w_key, w_value, w_out, state_in, grad_out):
@@ -47,8 +47,7 @@
     local_kv = jnp.einsum(
         "thd,the->hde", key_heads, value_heads, preferred_element_type=jnp.float32
     )
-    empty_state = jnp.zeros_like(local_kv)
-    earlier = carried_in(local_kv, "seq", add_states, empty_state, False)
+    earlier, _, _ = scanned(local_kv, "seq")
     state_before = state_in + earlier
     row_ids = lax.broadcasted_iota(jnp.int32, (shard_len, shard_len), 0)
     col_ids = lax.broadcasted_iota(jnp.int32, (shard_len, shard_len), 1)
@@ -75,10 +74,11 @@
     d_normed = d_normed.reshape(shard_len, head_count, head_width)
     d_attn = inverse * (d_normed - normed * jnp.mean(d_normed * normed, axis=-1, keepdims=True))
     local_adj = jnp.einsum("thd,the->hde", query_full, d_attn, precision=HIGH)
-    later = carried_in(local_adj, "seq", add_states, empty_state, True)
-    state_grad = lax.psum_scatter(
-        local_adj.astype(jnp.bfloat16), "seq", scatter_dimension=1, tiled=True
-    ).astype(jnp.float32)
+    _, later, adj_total = scanned(local_adj, "seq")
+    rows_per = head_width // lax.axis_size("seq")
+    state_grad = lax.dynamic_slice_in_dim(
+        adj_total, lax.axis_index("seq") * rows_per, rows_per, axis=1
+    )
     mixed_s = jnp.where(mask, jnp.einsum("the,she->hts", d_attn, value_full, precision=HIGH), 0.0)
     grad_q = jnp.einsum("the,hde->thd", d_attn, state_before, precision=HIGH) + jnp.einsum(
         "hts,shd->thd", mixed_s, key_full, precision=HIGH

time: 688 us -> 522 us (0.76)
  waiting for transfers between devices: 537 us -> 377 us
  starting transfers between devices: 1.04 us -> 22 us
  other arithmetic: 21.8 us -> 7.63 us
  matrix products: 95.6 us -> 86.2 us
    reduce_scatter x1, waiting for transfers between devices: 79.3 us -> 0.01 us  [body(): lax.psum_scatter(query_part.astype(jnp.bfloat16), 'seq', scatter_dimensio...]
    all_gather x2 -> x0, waiting for transfers between devices: 71.6 us -> none  [carried_in(): gathered = lax.all_gather(array.astype(jnp.bfloat16), axis)]
    ppermute x0 -> x8, waiting for transfers between devices: none -> 38.2 us  [scanned(): other = lax.ppermute(total, axis, pairs)]
    all_gather x1, waiting for transfers between devices: 26.9 us -> 0.02 us  [body(): grad_all = lax.all_gather(grad_out, 'tp', axis=0, tiled=True)]
    ppermute x0 -> x8, starting transfers between devices: none -> 21.2 us  [scanned(): other = lax.ppermute(total, axis, pairs)]
    add x15 -> x8, other arithmetic: 14.5 us -> 1.61 us  [the longest x7 1.53 us: scanned(): total = total + other]
    reduce_scatter x1, waiting for transfers between devices: 78.4 us -> 66.8 us  [body(): lax.psum_scatter(out_part.astype(jnp.bfloat16), 'seq', scatter_dimension=...]
    unnamed x12 -> x8, waiting for transfers between devices: 8.77 us -> 1.48 us
  transfers between devices with their start and end apart: 11 -> 16, of which waited for: 11 -> 14; matrix products, arithmetic and copies ran while one was open for 15% -> 15% of each run, Pallas kernels for 0% -> 0%
where the time goes in v1:
time: 522 us; the launch traced here: 515 us
  waiting for transfers between devices  377 us (72%)
  matrix products  86.2 us (17%)
  starting transfers between devices  22 us (4%)
  between operations  14.8 us (3%)
  other arithmetic  7.63 us (1%)
  local copies, waits for them, and re-layouts  7.32 us (1%)
    reduce_scatter x1, waiting for transfers between devices, body(): lax.psum_scatter(value_part.astype(jnp.bfloat16), 'seq', scatter_dimensio...  78.6 us
    reduce_scatter x1, waiting for transfers between devices, body(): lax.psum_scatter(key_part.astype(jnp.bfloat16), 'seq', scatter_dimension=...  78.4 us
    reduce_scatter x1, waiting for transfers between devices, body(): lax.psum_scatter(out_part.astype(jnp.bfloat16), 'seq', scatter_dimension=...  66.8 us
    reduce_scatter x1, waiting for transfers between devices, body(): lax.psum_scatter((term + lax.dot_general(value_grad, w_value, COLS_CONTRA...  39.8 us
    ppermute x8, waiting for transfers between devices, scanned(): other = lax.ppermute(total, axis, pairs)  38.2 us
    reduce_scatter x1, waiting for transfers between devices, body(): lax.psum_scatter(jnp.dot(heads_out, w_out, preferred_element_type=jnp.flo...  38 us
    all_gather x1, waiting for transfers between devices, body(): rows_all = lax.all_gather(tokens, 'tp', axis=0, tiled=True)  35.6 us
    ppermute x8, starting transfers between devices, scanned(): other = lax.ppermute(total, axis, pairs)  21.2 us
  transfers between devices with their start and end apart: 16, of which 14 were waited for; matrix products, arithmetic and copies ran while one was open for 15% of the time, Pallas kernels for 0%

profile of v1, /device:TPU:0, one launch (start us, length us, event | category | flops | bytes accessed | tf_op | source)
XLA Modules:
  0.0 514.9 jit_solution(3716976327167864774)
XLA Ops:
  8.7 35.6 %all-gather.3.cloned.1.call-done = bf16[512,4096]{1,0:T(8,128)(2,1)} async-done(((bf16[64,4096]{1,0:T(8,128)(2,1)}), bf16[512,4096]{1,0:T(8,128)(2,1)}) %all-gather.3.cloned.1.call-update) | async-done | bytes 4194320 | tf_op jit(solution)/shard_map/all_gather | solution.py:32
  44.3 6.0 %convolution_convert_fusion.5 = bf16[512,512]{0,1:T(8,128)(2,1)S(1)} fusion(bf16[512,4096]{1,0:T(8,128)(2,1)} %all-gather.3.cloned.1.call-done, bf16[4096,512]{1,0:T(8,128)(2,1)} %param.9), kind=kOutput, calls=%fused_computation.34 | convolution fusion | flops 2147745792 | bytes 8912896 | tf_op jit(solution)/shard_map/dot_general | solution.py:39
  54.6 6.9 %collective-permute-done = f32[4,128,128]{2,1,0:T(8,128)S(1)} collective-permute-done((f32[4,128,128]{2,1,0:T(8,128)S(1)}, f32[4,128,128]{2,1,0:T(8,128)S(1)}, u32[]{:S(2)}, u32[]{:S(2)}) %collective-permute-start) | collective-permute-done | bytes 262176 | tf_op jit(solution)/shard_map/ppermute | solution.py:20
  64.6 6.0 %convolution_convert_fusion.6 = bf16[512,512]{0,1:T(8,128)(2,1)S(1)} fusion(bf16[512,4096]{1,0:T(8,128)(2,1)} %all-gather.3.cloned.1.call-done, bf16[4096,512]{1,0:T(8,128)(2,1)} %param.8), kind=kOutput, calls=%fused_computation.35 | convolution fusion | flops 2147745792 | bytes 8912896 | tf_op jit(solution)/shard_map/dot_general | solution.py:38
  73.3 4.9 collective-permute-done.2
  87.6 5.9 %multiply_reduce_fusion = (f32[512,4]{0,1:T(4,128)S(1)}, f32[512,512]{0,1:T(8,128)S(1)}) fusion(f32[512,4,128]{0,2,1:T(8,128)S(1)} %get-tuple-element.17, f32[512,4]{0,1:T(4,128)S(1)} %add_rsqrt_fusion, bf16[512,4096]{1,0:T(8,128)(2,1)} %all-gather.5.cloned.1.call-done, bf16[512,4096]{1,0:T(8,128)(2,1)} %param.11), kind=kOutput, calls=%fused_computation.41 | convolution fusion | flops 2148268032 | bytes 10502144 | tf_op jit(solution)/shard_map/dot_general | solution.py:73
  101.1 4.5 fusion
  106.7 6.5 %convolution_convert_fusion = bf16[512,4096]{1,0:T(8,128)(2,1)} fusion(bf16[512,512]{0,1:T(8,128)(2,1)S(1)} %bitcast.92, bf16[512,4096]{1,0:T(8,128)(2,1)} %all-gather.5.cloned.1.call-done), kind=kOutput, calls=%fused_computation.1 | convolution fusion | flops 2149580800 | bytes 8912896 | tf_op jit(solution)/shard_map/dot_general | solution.py:70
  115.1 6.3 %collective-permute-done.4 = f32[4,128,128]{2,1,0:T(8,128)S(1)} collective-permute-done((f32[4,128,128]{2,1,0:T(8,128)S(1)}, f32[4,128,128]{2,1,0:T(8,128)S(1)}, u32[]{:S(2)}, u32[]{:S(2)}) %collective-permute-start.4) | collective-permute-done | bytes 262176 | tf_op jit(solution)/shard_map/ppermute | solution.py:20
  124.5 7.6 %collective-permute-done.5 = f32[4,128,128]{2,1,0:T(8,128)S(1)} collective-permute-done((f32[4,128,128]{2,1,0:T(8,128)S(1)}, f32[4,128,128]{2,1,0:T(8,128)S(1)}, u32[]{:S(2)}, u32[]{:S(2)}) %collective-permute-start.5) | collective-permute-done | bytes 262176 | tf_op jit(solution)/shard_map/ppermute | solution.py:20
  135.5 8.2 %collective-permute-done.6 = f32[4,128,128]{2,1,0:T(8,128)S(1)} collective-permute-done((f32[4,128,128]{2,1,0:T(8,128)S(1)}, f32[4,128,128]{2,1,0:T(8,128)S(1)}, u32[]{:S(2)}, u32[]{:S(2)}) %collective-permute-start.6) | collective-permute-done | bytes 262176 | tf_op jit(solution)/shard_map/ppermute | solution.py:20
  147.3 4.2 fusion.19
  154.3 4.3 fusion.1
  158.9 5.1 fusion.25
  165.5 4.4 fusion.2
  170.9 6.7 %convolution_convert_fusion.4 = bf16[512,4096]{1,0:T(8,128)(2,1)} fusion(bf16[512,512]{0,1:T(8,128)(2,1)S(1)} %bitcast.93, bf16[512,4096]{1,0:T(8,128)(2,1)} %param.11), kind=kOutput, calls=%fused_computation.5 | convolution fusion | flops 2149580800 | bytes 8912896 | tf_op jit(solution)/shard_map/dot_general | solution.py:64
  178.7 4.7 fusion.38
  183.5 5.7 %fusion.40 = f32[512,4096]{1,0:T(8,128)} fusion(bf16[512,512]{0,1:T(8,128)(2,1)S(1)} %bitcast.97, bf16[4096,512]{1,0:T(8,128)(2,1)S(1)} %copy-done.5), kind=kOutput, calls=%fused_computation.63 | convolution fusion | flops 2147483648 | bytes 13107200 | tf_op jit(solution)/shard_map/dot_general | solution.py:96
  189.2 7.8 %add_convert_fusion = bf16[512,4096]{1,0:T(8,128)(2,1)} fusion(f32[512,4096]{1,0:T(8,128)S(1)} %fusion.38, f32[512,4096]{1,0:T(8,128)} %fusion.40, bf16[512,512]{0,1:T(8,128)(2,1)S(1)} %bitcast.99, bf16[4096,512]{1,0:T(8,128)(2,1)S(1)} %copy-done.7), kind=kOutput, calls=%fused_computation | convolution fusion | flops 2153775104 | bytes 25690112 | tf_op jit(solution)/shard_map/dot_general | solution.py:102
  200.3 66.8 %reduce-scatter.17.cloned.1.call-done = bf16[512,256]{1,0:T(8,128)(2,1)} async-done(((bf16[512,4096]{1,0:T(8,128)(2,1)}), bf16[512,256]{1,0:T(8,128)(2,1)}) %reduce-scatter.17.cloned.1.call-update) | async-done | bytes 262160 | tf_op jit(solution)/shard_map/reduce_scatter | solution.py:129
  268.9 78.4 %reduce-scatter.13.cloned.1.call-done = bf16[256,512]{0,1:T(8,128)(2,1)} async-done(((bf16[4096,512]{0,1:T(8,128)(2,1)}), bf16[256,512]{0,1:T(8,128)(2,1)}) %reduce-scatter.13.cloned.1.call-update) | async-done | bytes 262160 | tf_op jit(solution)/shard_map/reduce_scatter | solution.py:123
  349.3 78.6 %reduce-scatter.15.cloned.1.call-done = bf16[256,512]{0,1:T(8,128)(2,1)} async-done(((bf16[4096,512]{0,1:T(8,128)(2,1)}), bf16[256,512]{0,1:T(8,128)(2,1)}) %reduce-scatter.15.cloned.1.call-update) | async-done | bytes 262160 | tf_op jit(solution)/shard_map/reduce_scatter | solution.py:126
  430.0 38.0 %reduce-scatter.7.cloned.1.call-done = bf16[64,4096]{1,0:T(8,128)(2,1)} async-done(((bf16[512,4096]{1,0:T(8,128)(2,1)}), bf16[64,4096]{1,0:T(8,128)(2,1)}) %reduce-scatter.7.cloned.1.call-update) | async-done | bytes 524304 | tf_op jit(solution)/shard_map/reduce_scatter | solution.py:63
  468.0 39.8 %reduce-scatter.9.cloned.1.call-done = bf16[64,4096]{1,0:T(8,128)(2,1)} async-done(((bf16[512,4096]{1,0:T(8,128)(2,1)}), bf16[64,4096]{1,0:T(8,128)(2,1)}) %reduce-scatter.9.cloned.1.call-update) | async-done | bytes 524304 | tf_op jit(solution)/shard_map/reduce_scatter | solution.py:99
  (110 shorter events, 57.2 us)
Async XLA Ops:
  7.2 37.1 %all-gather.3.cloned.1.call-start = ((), (), s32[]{:S(2)}) async-start(), calls=%async_computation.6 | async-start | bytes 4718592 | tf_op jit(solution)/shard_map/all_gather | solution.py:32
  7.9 79.7 %all-gather.5.cloned.1.call-start = ((), (), s32[]{:S(2)}) async-start(), calls=%async_computation.8 | async-start | bytes 4718592 | tf_op jit(solution)/shard_map/all_gather | solution.py:69
  8.6 189.7 %reduce-scatter.11.cloned.1.call-start = ((), (), s32[]{:S(2)}) async-start(), calls=%async_computation.10 | async-start | bytes 4456448 | tf_op jit(solution)/shard_map/reduce_scatter | solution.py:120
  52.7 29.3 %copy-start.2 = (bf16[512,512]{0,1:T(8,128)(2,1)}, bf16[512,512]{0,1:T(8,128)(2,1)S(1)}, u32[]{:S(2)}) copy-start(bf16[512,512]{0,1:T(8,128)(2,1)S(1)} %convolution_convert_fusion.7) | copy-start | bytes 1572868
  53.0 8.5 %collective-permute-start = (f32[4,128,128]{2,1,0:T(8,128)S(1)}, f32[4,128,128]{2,1,0:T(8,128)S(1)}, u32[]{:S(2)}, u32[]{:S(2)}) collective-permute-start(f32[4,128,128]{2,1,0:T(8,128)S(1)} %fusion.36), channel_id=1, source_target_pairs={{0,8},{8,0},{16,24},{24,16},{32,40},{40,32},{48,56},{56,48},{64,72... | collective-permute-start | bytes 786440 | tf_op jit(solution)/shard_map/ppermute | solution.py:20
  61.6 9.3 %collective-permute-start.1 = (f32[4,128,128]{2,1,0:T(8,128)S(1)}, f32[4,128,128]{2,1,0:T(8,128)S(1)}, u32[]{:S(2)}, u32[]{:S(2)}) collective-permute-start(f32[4,128,128]{2,1,0:T(8,128)S(1)} %add.90), channel_id=1, source_target_pairs={{0,16},{8,24},{16,0},{24,8},{32,48},{40,56},{48,32},{56,40},{64,80... | collective-permute-start | bytes 786440 | tf_op jit(solution)/shard_map/ppermute | solution.py:20
  70.9 7.3 %collective-permute-start.2 = (f32[4,128,128]{2,1,0:T(8,128)S(1)}, f32[4,128,128]{2,1,0:T(8,128)S(1)}, u32[]{:S(2)}, u32[]{:S(2)}) collective-permute-start(f32[4,128,128]{2,1,0:T(8,128)S(1)} %add.92), channel_id=1, source_target_pairs={{0,32},{8,40},{16,48},{24,56},{32,0},{40,8},{48,16},{56,24},{64,96... | collective-permute-start | bytes 786440 | tf_op jit(solution)/shard_map/ppermute | solution.py:20
  73.3 13.5 %copy-start = (f32[4,512,512]{2,1,0:T(8,128)}, f32[4,512,512]{2,1,0:T(8,128)S(1)}, u32[]{:S(2)}) copy-start(f32[4,512,512]{2,1,0:T(8,128)S(1)} %fusion.35) | copy-start | bytes 12582916
  73.3 13.4 %copy-start.20 = (f32[4,128,128]{2,1,0:T(8,128)S(1)}, f32[4,128,128]{2,1,0:T(8,128)}, u32[]{:S(2)}) copy-start(f32[4,128,128]{2,1,0:T(8,128)} %param.12) | copy-start | bytes 786436
  78.3 8.5 %collective-permute-start.3 = (f32[4,128,128]{2,1,0:T(8,128)S(1)}, f32[4,128,128]{2,1,0:T(8,128)S(1)}, u32[]{:S(2)}, u32[]{:S(2)}) collective-permute-start(f32[4,128,128]{2,1,0:T(8,128)S(1)} %add.94), channel_id=1, source_target_pairs={{0,64},{8,72},{16,80},{24,88},{32,96},{40,104},{48,112},{56,120},{... | collective-permute-start | bytes 786440 | tf_op jit(solution)/shard_map/ppermute | solution.py:20
  87.6 7.0 %copy-start.3 = (bf16[512,512]{0,1:T(8,128)(2,1)S(1)}, bf16[512,512]{0,1:T(8,128)(2,1)}, u32[]{:S(2)}) copy-start(bf16[512,512]{0,1:T(8,128)(2,1)} %copy-done.2) | copy-start | bytes 1572868
  105.7 161.4 %reduce-scatter.17.cloned.1.call-start = ((), (), s32[]{:S(2)}) async-start(), calls=%async_computation.13 | async-start | bytes 4456448 | tf_op jit(solution)/shard_map/reduce_scatter | solution.py:129
  113.2 234.1 %reduce-scatter.13.cloned.1.call-start = ((), (), s32[]{:S(2)}) async-start(), calls=%async_computation.11 | async-start | bytes 4456448 | tf_op jit(solution)/shard_map/reduce_scatter | solution.py:123
  113.9 7.5 %collective-permute-start.4 = (f32[4,128,128]{2,1,0:T(8,128)S(1)}, f32[4,128,128]{2,1,0:T(8,128)S(1)}, u32[]{:S(2)}, u32[]{:S(2)}) collective-permute-start(f32[4,128,128]{2,1,0:T(8,128)S(1)} %fusion.39), channel_id=1, source_target_pairs={{0,8},{8,0},{16,24},{24,16},{32,40},{40,32},{48,56},{56,48},{64,72... | collective-permute-start | bytes 786440 | tf_op jit(solution)/shard_map/ppermute | solution.py:20
  121.5 10.6 %collective-permute-start.5 = (f32[4,128,128]{2,1,0:T(8,128)S(1)}, f32[4,128,128]{2,1,0:T(8,128)S(1)}, u32[]{:S(2)}, u32[]{:S(2)}) collective-permute-start(f32[4,128,128]{2,1,0:T(8,128)S(1)} %add.102), channel_id=1, source_target_pairs={{0,16},{8,24},{16,0},{24,8},{32,48},{40,56},{48,32},{56,40},{64,80... | collective-permute-start | bytes 786440 | tf_op jit(solution)/shard_map/ppermute | solution.py:20
  132.1 21.5 %copy-start.4 = (bf16[512,512]{0,1:T(8,128)(2,1)S(1)}, bf16[512,512]{0,1:T(8,128)(2,1)}, u32[]{:S(2)}) copy-start(bf16[512,512]{0,1:T(8,128)(2,1)} %copy-done.2) | copy-start | bytes 1572868
  132.1 11.6 %collective-permute-start.6 = (f32[4,128,128]{2,1,0:T(8,128)S(1)}, f32[4,128,128]{2,1,0:T(8,128)S(1)}, u32[]{:S(2)}, u32[]{:S(2)}) collective-permute-start(f32[4,128,128]{2,1,0:T(8,128)S(1)} %add.104), channel_id=1, source_target_pairs={{0,32},{8,40},{16,48},{24,56},{32,0},{40,8},{48,16},{56,24},{64,96... | collective-permute-start | bytes 786440 | tf_op jit(solution)/shard_map/ppermute | solution.py:20
  143.8 10.5 %copy-start.18 = (f32[4,128,128]{2,1,0:T(8,128)}, f32[4,128,128]{2,1,0:T(8,128)S(1)}, u32[]{:S(2)}) copy-start(f32[4,128,128]{2,1,0:T(8,128)S(1)} %add.106) | copy-start | bytes 786436
  143.8 10.5 %copy-start.23 = (bf16[512,4096]{1,0:T(8,128)(2,1)S(1)}, bf16[512,4096]{1,0:T(8,128)(2,1)}, u32[]{:S(2)}) copy-start(bf16[512,4096]{1,0:T(8,128)(2,1)} %all-gather.3.cloned.1.call-done) | copy-start | bytes 12582916
  143.8 9.8 %collective-permute-start.7 = (f32[4,128,128]{2,1,0:T(8,128)S(1)}, f32[4,128,128]{2,1,0:T(8,128)S(1)}, u32[]{:S(2)}, u32[]{:S(2)}) collective-permute-start(f32[4,128,128]{2,1,0:T(8,128)S(1)} %add.106), channel_id=1, source_target_pairs={{0,64},{8,72},{16,80},{24,88},{32,96},{40,104},{48,112},{56,120},{... | collective-permute-start | bytes 786440 | tf_op jit(solution)/shard_map/ppermute | solution.py:20
  158.6 269.3 %reduce-scatter.15.cloned.1.call-start = ((), (), s32[]{:S(2)}) async-start(), calls=%async_computation.12 | async-start | bytes 4456448 | tf_op jit(solution)/shard_map/reduce_scatter | solution.py:126
  158.9 6.6 %copy-start.24 = (bf16[512,4096]{1,0:T(8,128)(2,1)S(1)}, bf16[512,4096]{1,0:T(8,128)(2,1)}, u32[]{:S(2)}) copy-start(bf16[512,4096]{1,0:T(8,128)(2,1)} %all-gather.3.cloned.1.call-done) | copy-start | bytes 12582916
  169.9 298.1 %reduce-scatter.7.cloned.1.call-start = ((), (), s32[]{:S(2)}) async-start(), calls=%async_computation.7 | async-start | bytes 4718592 | tf_op jit(solution)/shard_map/reduce_scatter | solution.py:63
  177.7 330.2 %reduce-scatter.9.cloned.1.call-start = ((), (), s32[]{:S(2)}) async-start(), calls=%async_computation.9 | async-start | bytes 4718592 | tf_op jit(solution)/shard_map/reduce_scatter | solution.py:99
  (17 other events, 55.8 us)
Sparse Core Ops, SparseCore 0:
  9.7 34.5 all-gather.2
  46.0 32.0 all-gather.4
  105.8 80.6 reduce-scatter.10
  190.0 77.0 reduce-scatter.16
  270.3 76.9 reduce-scatter.12
  350.9 77.0 reduce-scatter.14
  430.9 36.9 reduce-scatter.6
  470.9 36.8 reduce-scatter.8
